TPU v7x, 128 devices: a whole 4x4x4 slice. The times are simulated.
128 devices in a mesh: wide: 16 (over x, y_hi, core), narrow: 8 (over z, y_lo).
Axes of the slice: x: 4, y: 4 (y_hi: 2, y_lo: 2; y = y_hi * 2 + y_lo), z: 4, core: 2. Of those that a mesh axis runs over, the one named last changes fastest.
Arguments:
- hidden_in: bfloat16 [128, 8192], P('narrow', 'wide'), may hold values from -75 to 75
- lengths: int32 [128], P('wide'), may hold values from 32 to 8192, as said below
- kv_cache: bfloat16 [2, 2, 152576, 1024], P(None, None, 'wide', 'narrow'), may hold values from -210 to 210, as said below
- qkv_weight: bfloat16 [8192, 8, 1280], P('wide', 'narrow'), may hold values from -0.0625 to 0.0625
- o_weight: bfloat16 [8192, 8192], P('narrow', 'wide'), may hold values from -0.0625 to 0.0625
- gate_up: bfloat16 [8192, 2, 28672], P('wide', None, 'narrow'), may hold values from -0.0625 to 0.0625
- down_weight: bfloat16 [28672, 8192], P('narrow', 'wide'), may hold values from -0.03125 to 0.03125
- attn_gain: bfloat16 [8192], P('wide'), may hold values from 0.099609375 to 1.8984375
- mlp_gain: bfloat16 [8192], P('wide'), may hold values from 0.099609375 to 1.8984375
Outputs:
- hidden_out: bfloat16 [128, 8192], P('narrow', 'wide')
- new_entries: bfloat16 [2, 2, 128, 1024], P(None, None, 'wide', 'narrow')
Inputs may be any that keep to these rules, and one draw needn't show every extreme that they name: Exactly 8 requests have 8192 cached tokens, no two in the same aligned block of 8 requests; every other request has 32 to 192. The lengths of each aligned block of 8 requests sum to at most 9536, and those of one block to exactly 9536. `kv_cache`: cache positions that no request owns hold no live entries.
All inputs are finite; a program needn't handle non-finite values.
Results may differ from a plain program's by a relative error of at most 0.017.
Values may be sent and summed in bfloat16 or wider, within the bound.
No kernel may reach another device: no remote copies, remote signals or barrier semaphores. Data moves between devices by JAX's collectives and lax.ppermute only.
A program may use at most 128 MiB of HBM per device.

v0:
```python
import math
import jax
import jax.numpy as jnp
from jax import lax
from jax.sharding import PartitionSpec as P

D = 8192
HD = 128
LAYERS = 2
EPSILON = 1e-05
ROPE_BASE = 500000.0


def copy_for_each(shard, axis):
    length = lax.axis_size(axis)
    return lax.all_to_all(
        jnp.broadcast_to(shard[None], (length, *shard.shape)), axis, 0, 0, tiled=True
    )


def of_everyone(shard, axis):
    return copy_for_each(shard, axis).sum(axis=0)


def laid_out(parts, dim):
    parts = jnp.moveaxis(parts, 0, dim)
    lengths = parts.shape
    return parts.reshape(*lengths[:dim], lengths[dim] * lengths[dim + 1], *lengths[dim + 2 :])


def gathered_copies(shard, axis, dim):
    parts = copy_for_each(shard, axis)
    return laid_out(parts, dim)


def in_blocks(shard, dim, length):
    before, after = (shard.shape[:dim], shard.shape[dim + 1 :])
    return jnp.moveaxis(shard.reshape(*before, length, -1, *after), dim, 0)


def summed_on_arrival(shard, axis, dim):
    parts = in_blocks(shard, dim, lax.axis_size(axis))
    arrived = lax.all_to_all(parts, axis, split_axis=0, concat_axis=0, tiled=True)
    return arrived.sum(axis=0)


def sent_and_summed(shard, axis, dim):
    length = lax.axis_size(axis)
    parts = lax.all_to_all(in_blocks(shard, dim, length), axis, 0, 0, tiled=True)
    return jnp.sum(parts.astype(jnp.float32), axis=0)


def scale_rows(floats, square_sum, gain):
    scaled = (
        floats * lax.rsqrt(square_sum / D + EPSILON)[:, None] * gain.astype(jnp.float32)[None, :]
    )
    return scaled.astype(jnp.bfloat16)


def norm_rows(stream, gain):
    floats = stream.astype(jnp.float32)
    square_sum = lax.psum(jnp.sum(floats * floats, axis=1), "wide")
    return lax.all_gather(scale_rows(floats, square_sum, gain), "narrow", axis=0, tiled=True)


def rotate_pairs(vectors, cosine, sine_table):
    half_dim = vectors.shape[-1] // 2
    first_half = vectors[..., :half_dim]
    second_half = vectors[..., half_dim:]
    return jnp.concatenate(
        [
            first_half * cosine - second_half * sine_table,
            second_half * cosine + first_half * sine_table,
        ],
        axis=-1,
    )


def rotary_tables(lengths, head_dim):
    half_dim = head_dim // 2
    inverse = jnp.exp(
        jnp.arange(half_dim, dtype=jnp.float32) * (-2.0 * math.log(ROPE_BASE) / head_dim)
    )
    angles = lengths.astype(jnp.float32)[:, None] * inverse[None, :]
    return (jnp.cos(angles), jnp.sin(angles))


def split_heads(projected, lengths, heads_kv, head_dim):
    row_count = projected.shape[0]
    grouped = projected.reshape(row_count, heads_kv, -1, head_dim)
    group_size = grouped.shape[2] - 2
    cosine, sine_table = rotary_tables(lengths, head_dim)
    rotated = rotate_pairs(
        grouped[:, :, : group_size + 1], cosine[:, None, None, :], sine_table[:, None, None, :]
    )
    queries = rotated[:, :, :group_size].astype(jnp.bfloat16)
    key_new = rotated[:, :, group_size].astype(jnp.bfloat16)
    value_new = grouped[:, :, group_size + 1].astype(jnp.bfloat16)
    return (queries, key_new, value_new)


def attend(queries, key_new, value_new, cached_keys, cached_values, lengths):
    row_count, heads_kv, group_size, head_dim = queries.shape
    slot_count = cached_keys.shape[0]
    score_scale = 1.0 / math.sqrt(head_dim)
    key_table = cached_keys.reshape(slot_count, heads_kv, head_dim)
    value_table = cached_values.reshape(slot_count, heads_kv, head_dim)
    starts = jnp.cumsum(lengths) - lengths
    position = jnp.arange(slot_count, dtype=jnp.int32)
    owned = (position[None, :] >= starts[:, None]) & (
        position[None, :] < (starts + lengths)[:, None]
    )
    scores = (
        jnp.einsum("rkgd,tkd->krgt", queries, key_table, preferred_element_type=jnp.float32)
        * score_scale
    )
    scores = jnp.where(owned[None, :, None, :], scores, -jnp.inf)
    own_score = (
        jnp.einsum("rkgd,rkd->krg", queries, key_new, preferred_element_type=jnp.float32)
        * score_scale
    )
    row_peak = jnp.maximum(jnp.max(scores, axis=3), own_score)
    weights = jnp.exp(scores - row_peak[..., None])
    own_weight = jnp.exp(own_score - row_peak)
    weight_sum = jnp.sum(weights, axis=3) + own_weight
    blended = jnp.einsum(
        "krgt,tkd->krgd",
        weights.astype(jnp.bfloat16),
        value_table,
        preferred_element_type=jnp.float32,
    )
    own_rounded = lax.optimization_barrier(own_weight.astype(jnp.bfloat16)).astype(jnp.float32)
    blended = blended + own_rounded[..., None] * jnp.transpose(value_new, (1, 0, 2))[
        :, :, None, :
    ].astype(jnp.float32)
    normalized = (blended / weight_sum[..., None]).astype(jnp.bfloat16)
    return jnp.transpose(normalized, (1, 0, 2, 3)).reshape(
        row_count, heads_kv * group_size * head_dim
    )


def on_device(
    hidden_in, lengths, kv_cache, qkv_weight, o_weight, gate_up, down_weight, attn_gain, mlp_gain
):
    width_dev = hidden_in.shape[1]
    heads_kv = qkv_weight.shape[1]
    flat_qkv = qkv_weight.reshape(width_dev, -1)
    stream = hidden_in
    entries = []
    for layer_index in range(LAYERS):
        normed = norm_rows(stream, attn_gain)
        own_qkv = lax.psum_scatter(
            jnp.dot(normed, flat_qkv, preferred_element_type=jnp.float32),
            "wide",
            scatter_dimension=0,
            tiled=True,
        )
        queries, key_new, value_new = split_heads(own_qkv, lengths, heads_kv, HD)
        own_rows = key_new.shape[0]
        entries.append(
            jnp.stack(
                [
                    key_new.reshape(own_rows, heads_kv * HD),
                    value_new.reshape(own_rows, heads_kv * HD),
                ]
            )
        )
        attended = attend(
            queries, key_new, value_new, kv_cache[layer_index, 0], kv_cache[layer_index, 1], lengths
        )
        heads_all = lax.all_gather(attended, "wide", axis=0, tiled=True)
        summed = lax.psum_scatter(
            jnp.dot(heads_all, o_weight, preferred_element_type=jnp.float32),
            "narrow",
            scatter_dimension=0,
            tiled=True,
        )
        stream = (stream.astype(jnp.float32) + summed).astype(jnp.bfloat16)
        normed = norm_rows(stream, mlp_gain)
        both_parts = jnp.einsum("rd,dkh->rkh", normed, gate_up, preferred_element_type=jnp.float32)
        own_rows_parts = lax.psum_scatter(
            both_parts.astype(jnp.bfloat16), "wide", scatter_dimension=0, tiled=True
        ).astype(jnp.float32)
        activated = (jax.nn.silu(own_rows_parts[:, 0]) * own_rows_parts[:, 1]).astype(jnp.bfloat16)
        partial_down = jnp.dot(
            lax.all_gather(activated, "wide", axis=0, tiled=True),
            down_weight,
            preferred_element_type=jnp.float32,
        )
        summed = lax.psum_scatter(partial_down, "narrow", scatter_dimension=0, tiled=True)
        stream = (stream.astype(jnp.float32) + summed).astype(jnp.bfloat16)
    return (stream, jnp.stack(entries))


def solution(mesh):
    return jax.shard_map(
        on_device,
        mesh=mesh,
        in_specs=(
            P("narrow", "wide"),
            P("wide"),
            P(None, None, "wide", "narrow"),
            P("wide", "narrow", None),
            P("narrow", "wide"),
            P("wide", None, "narrow"),
            P("narrow", "wide"),
            P("wide"),
            P("wide"),
        ),
        out_specs=(P("narrow", "wide"), P(None, None, "wide", "narrow")),
        check_vma=False,
    )
```

profile of v0, /device:TPU:0, one launch (start us, length us, event | category | flops | bytes accessed | tf_op | source)
XLA Modules:
  0.0 797.2 jit_solution(17397242631848850265)
XLA Ops:
  7.2 0.9 fusion.91
  8.2 38.1 %psum.28 = f32[16]{0:T(128)S(1)} all-reduce(f32[16]{0:T(128)S(1)} %fusion.91), channel_id=1, replica_groups=mesh['wide'=16,'narrow'=8] {'wide'}, use_global_device_ids=true, to_apply=%region_2.0 | all-reduce | flops 16 | bytes 128 | tf_op jit(solution)/shard_map/psum | solution.py:62
  46.3 0.7 convert_element_type.205
  46.9 0.8 fusion.93
  47.7 29.7 %all_gather.24 = bf16[128,512]{1,0:T(8,128)(2,1)S(1)} all-gather(bf16[16,512]{1,0:T(8,128)(2,1)S(1)} %fusion.93), channel_id=1, replica_groups=mesh['wide'=16,'narrow'=8] {'narrow'}, dimensions={0}, use_global_device_ids=true | all-gather | bytes 147456 | tf_op jit(solution)/shard_map/all_gather | solution.py:63
  77.4 1.2 fusion.34
  79.1 61.7 %reduce-scatter.13.cloned.1.call-done = f32[8,1280]{1,0:T(8,128)} async-done(((f32[128,1280]{1,0:T(8,128)}), f32[8,1280]{1,0:T(8,128)}) %reduce-scatter.13.cloned.1.call-update) | async-done | bytes 40976 | tf_op jit(solution)/shard_map/reduce_scatter | solution.py:152
  140.9 0.7 fusion.121
  141.5 0.9 fusion.127
  142.8 2.7 fusion.128
  146.1 2.4 fusion.70
  148.6 22.3 %all_gather.25 = bf16[128,1024]{1,0:T(8,128)(2,1)S(1)} all-gather(bf16[8,1024]{1,0:T(8,128)(2,1)S(1)} %bitcast.162), channel_id=1, replica_groups=mesh['wide'=16,'narrow'=8] {'wide'}, dimensions={0}, use_global_device_ids=true | all-gather | bytes 278528 | tf_op jit(solution)/shard_map/all_gather | solution.py:171
  170.9 1.0 fusion.130
  172.0 35.1 %reduce-scatter.15.cloned.1.call-done = f32[16,512]{1,0:T(8,128)} async-done(((f32[128,512]{1,0:T(8,128)}), f32[16,512]{1,0:T(8,128)}) %reduce-scatter.15.cloned.1.call-update) | async-done | bytes 32784 | tf_op jit(solution)/shard_map/reduce_scatter | solution.py:172
  207.1 0.9 fusion.95
  208.0 33.2 %psum.29 = f32[16]{0:T(128)S(1)} all-reduce(f32[16]{0:T(128)S(1)} %get-tuple-element.6), channel_id=1, replica_groups=mesh['wide'=16,'narrow'=8] {'wide'}, use_global_device_ids=true, to_apply=%region_8.9 | all-reduce | flops 16 | bytes 128 | tf_op jit(solution)/shard_map/psum | solution.py:62
  241.2 28.3 %all_gather.26 = bf16[128,512]{1,0:T(8,128)(2,1)S(1)} all-gather(bf16[16,512]{1,0:T(8,128)(2,1)S(1)} %fusion.97), channel_id=1, replica_groups=mesh['wide'=16,'narrow'=8] {'narrow'}, dimensions={0}, use_global_device_ids=true | all-gather | bytes 147456 | tf_op jit(solution)/shard_map/all_gather | solution.py:63
  269.5 4.2 fusion.15
  273.7 1.4 copy.60
  275.3 63.8 %reduce-scatter.25.cloned.1.call-done = bf16[8,7168]{1,0:T(8,128)(2,1)} async-done(((bf16[128,7168]{1,0:T(8,128)(2,1)}), bf16[8,7168]{1,0:T(8,128)(2,1)}) %reduce-scatter.25.cloned.1.call-update) | async-done | bytes 114704
  339.0 0.9 convert_element_type.222
  340.0 24.2 %all_gather.27 = bf16[128,3584]{1,0:T(8,128)(2,1)S(1)} all-gather(bf16[8,3584]{1,0:T(8,128)(2,1)S(1)} %fusion.86), channel_id=1, replica_groups=mesh['wide'=16,'narrow'=8] {'wide'}, dimensions={0}, use_global_device_ids=true | all-gather | bytes 974848 | tf_op jit(solution)/shard_map/all_gather | solution.py:186
  364.2 3.4 fusion.131
  367.6 35.6 %reduce-scatter.17.cloned.1.call-done = f32[16,512]{1,0:T(8,128)} async-done(((f32[128,512]{1,0:T(8,128)}), f32[16,512]{1,0:T(8,128)}) %reduce-scatter.17.cloned.1.call-update) | async-done | bytes 32784 | tf_op jit(solution)/shard_map/reduce_scatter | solution.py:190
  403.2 0.9 fusion.99
  404.1 33.2 %psum.30 = f32[16]{0:T(128)S(1)} all-reduce(f32[16]{0:T(128)S(1)} %get-tuple-element.4), channel_id=1, replica_groups=mesh['wide'=16,'narrow'=8] {'wide'}, use_global_device_ids=true, to_apply=%region_12.13 | all-reduce | flops 16 | bytes 128 | tf_op jit(solution)/shard_map/psum | solution.py:62
  437.4 28.3 %all_gather.28 = bf16[128,512]{1,0:T(8,128)(2,1)S(1)} all-gather(bf16[16,512]{1,0:T(8,128)(2,1)S(1)} %fusion.101), channel_id=1, replica_groups=mesh['wide'=16,'narrow'=8] {'narrow'}, dimensions={0}, use_global_device_ids=true | all-gather | bytes 147456 | tf_op jit(solution)/shard_map/all_gather | solution.py:63
  465.7 1.2 fusion.32
  467.0 59.8 %reduce-scatter.19.cloned.1.call-done = f32[8,1280]{1,0:T(8,128)} async-done(((f32[128,1280]{1,0:T(8,128)}), f32[8,1280]{1,0:T(8,128)}) %reduce-scatter.19.cloned.1.call-update) | async-done | bytes 40976 | tf_op jit(solution)/shard_map/reduce_scatter | solution.py:152
  526.7 0.7 fusion.122
  527.4 0.9 fusion.126
  528.5 2.7 fusion.129
  532.0 2.3 fusion.75
  534.3 22.3 %all_gather.29 = bf16[128,1024]{1,0:T(8,128)(2,1)S(1)} all-gather(bf16[8,1024]{1,0:T(8,128)(2,1)S(1)} %bitcast.163), channel_id=1, replica_groups=mesh['wide'=16,'narrow'=8] {'wide'}, dimensions={0}, use_global_device_ids=true | all-gather | bytes 278528 | tf_op jit(solution)/shard_map/all_gather | solution.py:171
  556.6 1.0 fusion.132
  557.7 35.2 %reduce-scatter.21.cloned.1.call-done = f32[16,512]{1,0:T(8,128)} async-done(((f32[128,512]{1,0:T(8,128)}), f32[16,512]{1,0:T(8,128)}) %reduce-scatter.21.cloned.1.call-update) | async-done | bytes 32784 | tf_op jit(solution)/shard_map/reduce_scatter | solution.py:172
  592.9 0.9 fusion.103
  593.8 33.2 %psum.31 = f32[16]{0:T(128)S(1)} all-reduce(f32[16]{0:T(128)S(1)} %get-tuple-element.2), channel_id=1, replica_groups=mesh['wide'=16,'narrow'=8] {'wide'}, use_global_device_ids=true, to_apply=%region_18.19 | all-reduce | flops 16 | bytes 128 | tf_op jit(solution)/shard_map/psum | solution.py:62
  627.0 28.3 %all_gather.30 = bf16[128,512]{1,0:T(8,128)(2,1)S(1)} all-gather(bf16[16,512]{1,0:T(8,128)(2,1)S(1)} %fusion.105), channel_id=1, replica_groups=mesh['wide'=16,'narrow'=8] {'narrow'}, dimensions={0}, use_global_device_ids=true | all-gather | bytes 147456 | tf_op jit(solution)/shard_map/all_gather | solution.py:63
  655.3 4.2 fusion.12
  659.5 1.4 copy.61
  661.0 63.8 %reduce-scatter.27.cloned.1.call-done = bf16[8,7168]{1,0:T(8,128)(2,1)} async-done(((bf16[128,7168]{1,0:T(8,128)(2,1)}), bf16[8,7168]{1,0:T(8,128)(2,1)}) %reduce-scatter.27.cloned.1.call-update) | async-done | bytes 114704
  724.8 0.9 convert_element_type.240
  725.8 24.2 %all_gather.31 = bf16[128,3584]{1,0:T(8,128)(2,1)S(1)} all-gather(bf16[8,3584]{1,0:T(8,128)(2,1)S(1)} %fusion.84), channel_id=1, replica_groups=mesh['wide'=16,'narrow'=8] {'wide'}, dimensions={0}, use_global_device_ids=true | all-gather | bytes 974848 | tf_op jit(solution)/shard_map/all_gather | solution.py:186
  750.0 3.4 fusion.133
  753.4 0.6 pad_maximum_fusion
  754.0 35.0 %reduce-scatter.23.cloned.1.call-done = f32[16,512]{1,0:T(8,128)} async-done(((f32[128,512]{1,0:T(8,128)}), f32[16,512]{1,0:T(8,128)}) %reduce-scatter.23.cloned.1.call-update) | async-done | bytes 32784 | tf_op jit(solution)/shard_map/reduce_scatter | solution.py:190
  789.0 1.4 fusion.106
  (63 shorter events, 3.1 us)
Async XLA Ops:
  7.2 70.2 %copy-start = (bf16[512,1,1280]{2,0,1:T(8,128)(2,1)S(1)}, bf16[512,1,1280]{2,0,1:T(8,128)(2,1)}, u32[]{:S(2)}) copy-start(bf16[512,1,1280]{2,0,1:T(8,128)(2,1)} %param.12) | copy-start | bytes 3932164
  7.2 71.5 %copy-start.4 = (s32[8]{0:T(128)S(1)}, s32[8]{0:T(128)}, u32[]{:S(2)}) copy-start(s32[8]{0:T(128)} %param.10) | copy-start | bytes 100
  7.2 133.7 %reduce-scatter.13.cloned.1.call-start = ((), (), s32[]{:S(2)}) async-start(), calls=%async_computation.8 | async-start | bytes 696320 | tf_op jit(solution)/shard_map/reduce_scatter | solution.py:152
  78.6 128.5 %reduce-scatter.15.cloned.1.call-start = ((), (), s32[]{:S(2)}) async-start(), calls=%async_computation.9 | async-start | bytes 294912 | tf_op jit(solution)/shard_map/reduce_scatter | solution.py:172
  146.1 24.8 %copy-start.1 = (bf16[1024,512]{1,0:T(8,128)(2,1)S(1)}, bf16[1024,512]{1,0:T(8,128)(2,1)}, u32[]{:S(2)}) copy-start(bf16[1024,512]{1,0:T(8,128)(2,1)} %param.13) | copy-start | bytes 3145732
  146.1 25.8 %copy-start.3 = (bf16[512]{0:T(512)(128)(2,1)S(1)}, bf16[512]{0:T(512)(128)(2,1)}, u32[]{:S(2)}) copy-start(bf16[512]{0:T(512)(128)(2,1)} %param.17) | copy-start | bytes 3076
  146.1 61.0 %copy-start.2 = (bf16[16,512]{1,0:T(8,128)(2,1)S(1)}, bf16[16,512]{1,0:T(8,128)(2,1)}, u32[]{:S(2)}) copy-start(bf16[16,512]{1,0:T(8,128)(2,1)} %param.9) | copy-start | bytes 49156
  171.9 167.1 %reduce-scatter.25.cloned.1.call-start = ((), (), s32[]{:S(2)}) async-start(), calls=%async_computation.14 | async-start | bytes 1949696
  275.2 128.0 %reduce-scatter.17.cloned.1.call-start = ((), (), s32[]{:S(2)}) async-start(), calls=%async_computation.10 | async-start | bytes 294912 | tf_op jit(solution)/shard_map/reduce_scatter | solution.py:190
  367.6 159.2 %reduce-scatter.19.cloned.1.call-start = ((), (), s32[]{:S(2)}) async-start(), calls=%async_computation.11 | async-start | bytes 696320 | tf_op jit(solution)/shard_map/reduce_scatter | solution.py:152
  466.9 126.0 %reduce-scatter.21.cloned.1.call-start = ((), (), s32[]{:S(2)}) async-start(), calls=%async_computation.12 | async-start | bytes 294912 | tf_op jit(solution)/shard_map/reduce_scatter | solution.py:172
  557.7 167.1 %reduce-scatter.27.cloned.1.call-start = ((), (), s32[]{:S(2)}) async-start(), calls=%async_computation.15 | async-start | bytes 1949696
  661.0 128.0 %reduce-scatter.23.cloned.1.call-start = ((), (), s32[]{:S(2)}) async-start(), calls=%async_computation.13 | async-start | bytes 294912 | tf_op jit(solution)/shard_map/reduce_scatter | solution.py:190
Sparse Core Ops, SparseCore 0:
  78.7 62.0 reduce-scatter.12
  172.0 35.0 reduce-scatter.14
  275.3 63.6 reduce-scatter.24
  367.7 35.4 reduce-scatter.16
  467.0 59.6 reduce-scatter.18
  557.8 35.0 reduce-scatter.20
  661.1 63.6 reduce-scatter.26
  753.5 35.4 reduce-scatter.22
where the time goes:
time: 798 us; the launch traced here: 797 us
  waiting for transfers between devices  390 us (49%)
  blocking collectives  345 us (43%)
  matrix products  30.1 us (4%)
  between operations  14.3 us (2%)
  other arithmetic  12.5 us (2%)
    psum x4, blocking collectives, norm_rows(): square_sum = lax.psum(jnp.sum(floats * floats, axis=1), 'wide')  138 us
    unnamed x10, waiting for transfers between devices  128 us
    reduce_scatter x2, waiting for transfers between devices, on_device(): lax.psum_scatter(jnp.dot(normed, flat_qkv, preferred_element_type=jnp.flo...  122 us
    all_gather x4, blocking collectives, norm_rows(): lax.all_gather(scale_rows(floats, square_sum, gain), 'narrow', axis=0, ti...  115 us
    reduce_scatter x2, waiting for transfers between devices, on_device(): lax.psum_scatter(partial_down, 'narrow', scatter_dimension=0, tiled=True)  70.6 us
    reduce_scatter x2, waiting for transfers between devices, on_device(): lax.psum_scatter(jnp.dot(heads_all, o_weight, preferred_element_type=jnp....  70.3 us
    all_gather x2, blocking collectives, on_device(): lax.all_gather(activated, 'wide', axis=0, tiled=True)  48.3 us
    all_gather x2, blocking collectives, on_device(): heads_all = lax.all_gather(attended, 'wide', axis=0, tiled=True)  44.6 us
  transfers between devices with their start and end apart: 8, of which 8 were waited for; matrix products, arithmetic and copies ran while one was open for 0% of the time, Pallas kernels for 0%

commit v1 on v0

--- a/solution.py
+++ b/solution.py
@@ -9,6 +9,15 @@
 LAYERS = 2
 EPSILON = 1e-05
 ROPE_BASE = 500000.0
+supply_all_target_for = lambda page: jnp.concatenate(
+    jax.lax.all_to_all(
+        jnp.stack([page] * jax.lax.axis_size("narrow")),
+        axis_name="narrow",
+        concat_axis=0,
+        split_axis=0,
+    ),
+    axis=0,
+)
 
 
 def copy_for_each(shard, axis):
@@ -60,7 +69,7 @@
 def norm_rows(stream, gain):
     floats = stream.astype(jnp.float32)
     square_sum = lax.psum(jnp.sum(floats * floats, axis=1), "wide")
-    return lax.all_gather(scale_rows(floats, square_sum, gain), "narrow", axis=0, tiled=True)
+    return supply_all_target_for(scale_rows(floats, square_sum, gain))
 
 
 def rotate_pairs(vectors, cosine, sine_table):

time: 798 us -> 725 us (0.909)
  blocking collectives: 345 us -> 258 us
    all_gather x4 -> x0, blocking collectives: 115 us -> none  [norm_rows(): lax.all_gather(scale_rows(floats, square_sum, gain), 'narrow', axis=0, ti...]
    all_to_all x0 -> x3, blocking collectives: none -> 27.3 us  [jax.lax.all_to_all(jnp.stack([page] * jax.lax.axis_size('narrow')), axis_...]
  transfers between devices with their start and end apart: 8 -> 9, of which waited for: 8 -> 9; matrix products, arithmetic and copies ran while one was open for 0% -> 0% of each run, Pallas kernels for 0% -> 0%
where the time goes in v1:
time: 725 us; the launch traced here: 724 us
  waiting for transfers between devices  396 us (55%)
  blocking collectives  258 us (36%)
  matrix products  30.1 us (4%)
  between operations  14.3 us (2%)
  other arithmetic  13.9 us (2%)
    psum x4, blocking collectives, norm_rows(): square_sum = lax.psum(jnp.sum(floats * floats, axis=1), 'wide')  138 us
    unnamed x10, waiting for transfers between devices  129 us
    reduce_scatter x2, waiting for transfers between devices, on_device(): lax.psum_scatter(jnp.dot(normed, flat_qkv, preferred_element_type=jnp.flo...  121 us
    reduce_scatter x2, waiting for transfers between devices, on_device(): lax.psum_scatter(partial_down, 'narrow', scatter_dimension=0, tiled=True)  70.6 us
    reduce_scatter x2, waiting for transfers between devices, on_device(): lax.psum_scatter(jnp.dot(heads_all, o_weight, preferred_element_type=jnp....  70.4 us
    all_gather x2, blocking collectives, on_device(): lax.all_gather(activated, 'wide', axis=0, tiled=True)  48.3 us
    all_gather x2, blocking collectives, on_device(): heads_all = lax.all_gather(attended, 'wide', axis=0, tiled=True)  44.6 us
    all_to_all x3, blocking collectives, jax.lax.all_to_all(jnp.stack([page] * jax.lax.axis_size('narrow')), axis_...  27.3 us
  transfers between devices with their start and end apart: 9, of which 9 were waited for; matrix products, arithmetic and copies ran while one was open for 0% of the time, Pallas kernels for 0%

profile of v1, /device:TPU:0, one launch (start us, length us, event | category | flops | bytes accessed | tf_op | source)
XLA Modules:
  0.0 723.5 jit_solution(3692754149465778626)
XLA Ops:
  7.2 0.9 fusion.89
  8.1 38.1 %psum.28 = f32[16]{0:T(128)S(1)} all-reduce(f32[16]{0:T(128)S(1)} %fusion.89), channel_id=1, replica_groups=mesh['wide'=16,'narrow'=8] {'wide'}, use_global_device_ids=true, to_apply=%region_2.0 | all-reduce | flops 16 | bytes 128 | tf_op jit(solution)/shard_map/psum | solution.py:71
  46.2 0.7 convert_element_type.205
  46.9 0.8 fusion.91
  48.3 5.4 all-to-all-start
  53.8 0.8 reduce-window.8
  54.6 0.7 bitcast_subtract_fusion
  55.4 5.1 all-to-all-done
  60.5 1.2 fusion.34
  62.0 60.3 %reduce-scatter.13.cloned.1.call-done = f32[8,1280]{1,0:T(8,128)} async-done(((f32[128,1280]{1,0:T(8,128)}), f32[8,1280]{1,0:T(8,128)}) %reduce-scatter.13.cloned.1.call-update) | async-done | bytes 40976 | tf_op jit(solution)/shard_map/reduce_scatter | solution.py:161
  123.0 0.9 fusion.125
  124.2 2.7 fusion.126
  127.6 2.4 fusion.70
  130.0 22.3 %all_gather.12 = bf16[128,1024]{1,0:T(8,128)(2,1)S(1)} all-gather(bf16[8,1024]{1,0:T(8,128)(2,1)S(1)} %bitcast.170), channel_id=1, replica_groups=mesh['wide'=16,'narrow'=8] {'wide'}, dimensions={0}, use_global_device_ids=true | all-gather | bytes 278528 | tf_op jit(solution)/shard_map/all_gather | solution.py:180
  152.3 1.0 fusion.128
  153.4 35.2 %reduce-scatter.15.cloned.1.call-done = f32[16,512]{1,0:T(8,128)} async-done(((f32[128,512]{1,0:T(8,128)}), f32[16,512]{1,0:T(8,128)}) %reduce-scatter.15.cloned.1.call-update) | async-done | bytes 32784 | tf_op jit(solution)/shard_map/reduce_scatter | solution.py:181
  188.6 0.9 fusion.93
  189.5 33.2 %psum.29 = f32[16]{0:T(128)S(1)} all-reduce(f32[16]{0:T(128)S(1)} %get-tuple-element.6), channel_id=1, replica_groups=mesh['wide'=16,'narrow'=8] {'wide'}, use_global_device_ids=true, to_apply=%region_8.9 | all-reduce | flops 16 | bytes 128 | tf_op jit(solution)/shard_map/psum | solution.py:71
  222.8 9.1 %all_to_all.20 = bf16[8,16,512]{2,1,0:T(8,128)(2,1)S(1)} all-to-all(bf16[8,16,512]{2,1,0:T(8,128)(2,1)S(1)} %stack.19), channel_id=1, replica_groups=mesh['wide'=16,'narrow'=8] {'narrow'}, dimensions={0} | all-to-all | bytes 262144 | tf_op jit(solution)/shard_map/all_to_all | solution.py:13
  231.9 4.2 fusion.15
  236.1 1.4 copy.60
  237.6 64.5 %reduce-scatter.25.cloned.1.call-done = bf16[8,7168]{1,0:T(8,128)(2,1)} async-done(((bf16[128,7168]{1,0:T(8,128)(2,1)}), bf16[8,7168]{1,0:T(8,128)(2,1)}) %reduce-scatter.25.cloned.1.call-update) | async-done | bytes 114704
  302.1 0.9 convert_element_type.222
  303.1 24.2 %all_gather.13 = bf16[128,3584]{1,0:T(8,128)(2,1)S(1)} all-gather(bf16[8,3584]{1,0:T(8,128)(2,1)S(1)} %fusion.84), channel_id=1, replica_groups=mesh['wide'=16,'narrow'=8] {'wide'}, dimensions={0}, use_global_device_ids=true | all-gather | bytes 974848 | tf_op jit(solution)/shard_map/all_gather | solution.py:195
  327.3 3.4 fusion.129
  330.7 35.6 %reduce-scatter.17.cloned.1.call-done = f32[16,512]{1,0:T(8,128)} async-done(((f32[128,512]{1,0:T(8,128)}), f32[16,512]{1,0:T(8,128)}) %reduce-scatter.17.cloned.1.call-update) | async-done | bytes 32784 | tf_op jit(solution)/shard_map/reduce_scatter | solution.py:199
  366.4 0.9 fusion.97
  367.2 33.2 %psum.30 = f32[16]{0:T(128)S(1)} all-reduce(f32[16]{0:T(128)S(1)} %get-tuple-element.4), channel_id=1, replica_groups=mesh['wide'=16,'narrow'=8] {'wide'}, use_global_device_ids=true, to_apply=%region_12.13 | all-reduce | flops 16 | bytes 128 | tf_op jit(solution)/shard_map/psum | solution.py:71
  400.5 9.1 %all_to_all.21 = bf16[8,16,512]{2,1,0:T(8,128)(2,1)S(1)} all-to-all(bf16[8,16,512]{2,1,0:T(8,128)(2,1)S(1)} %stack.20), channel_id=1, replica_groups=mesh['wide'=16,'narrow'=8] {'narrow'}, dimensions={0} | all-to-all | bytes 262144 | tf_op jit(solution)/shard_map/all_to_all | solution.py:13
  409.6 1.2 fusion.32
  410.9 60.6 %reduce-scatter.19.cloned.1.call-done = f32[8,1280]{1,0:T(8,128)} async-done(((f32[128,1280]{1,0:T(8,128)}), f32[8,1280]{1,0:T(8,128)}) %reduce-scatter.19.cloned.1.call-update) | async-done | bytes 40976 | tf_op jit(solution)/shard_map/reduce_scatter | solution.py:161
  472.1 0.9 fusion.124
  473.3 2.7 fusion.127
  476.7 2.3 fusion.75
  479.1 22.3 %all_gather.14 = bf16[128,1024]{1,0:T(8,128)(2,1)S(1)} all-gather(bf16[8,1024]{1,0:T(8,128)(2,1)S(1)} %bitcast.171), channel_id=1, replica_groups=mesh['wide'=16,'narrow'=8] {'wide'}, dimensions={0}, use_global_device_ids=true | all-gather | bytes 278528 | tf_op jit(solution)/shard_map/all_gather | solution.py:180
  501.3 1.0 fusion.130
  502.4 35.2 %reduce-scatter.21.cloned.1.call-done = f32[16,512]{1,0:T(8,128)} async-done(((f32[128,512]{1,0:T(8,128)}), f32[16,512]{1,0:T(8,128)}) %reduce-scatter.21.cloned.1.call-update) | async-done | bytes 32784 | tf_op jit(solution)/shard_map/reduce_scatter | solution.py:181
  537.6 0.9 fusion.101
  538.5 33.2 %psum.31 = f32[16]{0:T(128)S(1)} all-reduce(f32[16]{0:T(128)S(1)} %get-tuple-element.2), channel_id=1, replica_groups=mesh['wide'=16,'narrow'=8] {'wide'}, use_global_device_ids=true, to_apply=%region_18.19 | all-reduce | flops 16 | bytes 128 | tf_op jit(solution)/shard_map/psum | solution.py:71
  571.8 9.1 %all_to_all.22 = bf16[8,16,512]{2,1,0:T(8,128)(2,1)S(1)} all-to-all(bf16[8,16,512]{2,1,0:T(8,128)(2,1)S(1)} %stack.21), channel_id=1, replica_groups=mesh['wide'=16,'narrow'=8] {'narrow'}, dimensions={0} | all-to-all | bytes 262144 | tf_op jit(solution)/shard_map/all_to_all | solution.py:13
  580.9 4.2 fusion.12
  585.1 1.4 copy.61
  586.7 64.5 %reduce-scatter.27.cloned.1.call-done = bf16[8,7168]{1,0:T(8,128)(2,1)} async-done(((bf16[128,7168]{1,0:T(8,128)(2,1)}), bf16[8,7168]{1,0:T(8,128)(2,1)}) %reduce-scatter.27.cloned.1.call-update) | async-done | bytes 114704
  651.2 0.9 convert_element_type.240
  652.2 24.2 %all_gather.15 = bf16[128,3584]{1,0:T(8,128)(2,1)S(1)} all-gather(bf16[8,3584]{1,0:T(8,128)(2,1)S(1)} %fusion.82), channel_id=1, replica_groups=mesh['wide'=16,'narrow'=8] {'wide'}, dimensions={0}, use_global_device_ids=true | all-gather | bytes 974848 | tf_op jit(solution)/shard_map/all_gather | solution.py:195
  676.3 3.4 fusion.131
  680.4 35.0 %reduce-scatter.23.cloned.1.call-done = f32[16,512]{1,0:T(8,128)} async-done(((f32[128,512]{1,0:T(8,128)}), f32[16,512]{1,0:T(8,128)}) %reduce-scatter.23.cloned.1.call-update) | async-done | bytes 32784 | tf_op jit(solution)/shard_map/reduce_scatter | solution.py:199
  715.3 1.4 fusion.104
  (66 shorter events, 5.5 us)
Async XLA Ops:
  7.2 53.3 %copy-start = (bf16[512,1,1280]{2,0,1:T(8,128)(2,1)S(1)}, bf16[512,1,1280]{2,0,1:T(8,128)(2,1)}, u32[]{:S(2)}) copy-start(bf16[512,1,1280]{2,0,1:T(8,128)(2,1)} %param.12) | copy-start | bytes 3932164
  48.3 12.1 %all-to-all-start = ((bf16[8,16,512]{2,1,0:T(8,128)(2,1)}), bf16[8,16,512]{2,1,0:T(8,128)(2,1)S(1)}, u32[]{:S(2)}, u32[]{:S(2)}) async-start(bf16[8,16,512]{2,1,0:T(8,128)(2,1)} %stack.18), calls=%async_computation | async-start | bytes 262144 | tf_op jit(solution)/shard_map/all_to_all | solution.py:13
  53.8 68.5 %reduce-scatter.13.cloned.1.call-start = ((), (), s32[]{:S(2)}) async-start(), calls=%async_computation.12 | async-start | bytes 696320 | tf_op jit(solution)/shard_map/reduce_scatter | solution.py:161
  61.7 127.0 %reduce-scatter.15.cloned.1.call-start = ((), (), s32[]{:S(2)}) async-start(), calls=%async_computation.13 | async-start | bytes 294912 | tf_op jit(solution)/shard_map/reduce_scatter | solution.py:181
  127.5 24.8 %copy-start.1 = (bf16[1024,512]{1,0:T(8,128)(2,1)S(1)}, bf16[1024,512]{1,0:T(8,128)(2,1)}, u32[]{:S(2)}) copy-start(bf16[1024,512]{1,0:T(8,128)(2,1)} %param.13) | copy-start | bytes 3145732
  127.6 25.8 %copy-start.3 = (bf16[512]{0:T(512)(128)(2,1)S(1)}, bf16[512]{0:T(512)(128)(2,1)}, u32[]{:S(2)}) copy-start(bf16[512]{0:T(512)(128)(2,1)} %param.17) | copy-start | bytes 3076
  127.6 61.1 %copy-start.2 = (bf16[16,512]{1,0:T(8,128)(2,1)S(1)}, bf16[16,512]{1,0:T(8,128)(2,1)}, u32[]{:S(2)}) copy-start(bf16[16,512]{1,0:T(8,128)(2,1)} %param.9) | copy-start | bytes 49156
  153.3 148.8 %reduce-scatter.25.cloned.1.call-start = ((), (), s32[]{:S(2)}) async-start(), calls=%async_computation.18 | async-start | bytes 1949696
  237.6 128.8 %reduce-scatter.17.cloned.1.call-start = ((), (), s32[]{:S(2)}) async-start(), calls=%async_computation.14 | async-start | bytes 294912 | tf_op jit(solution)/shard_map/reduce_scatter | solution.py:199
  330.7 140.8 %reduce-scatter.19.cloned.1.call-start = ((), (), s32[]{:S(2)}) async-start(), calls=%async_computation.15 | async-start | bytes 696320 | tf_op jit(solution)/shard_map/reduce_scatter | solution.py:161
  410.8 126.8 %reduce-scatter.21.cloned.1.call-start = ((), (), s32[]{:S(2)}) async-start(), calls=%async_computation.16 | async-start | bytes 294912 | tf_op jit(solution)/shard_map/reduce_scatter | solution.py:181
  502.4 148.8 %reduce-scatter.27.cloned.1.call-start = ((), (), s32[]{:S(2)}) async-start(), calls=%async_computation.19 | async-start | bytes 1949696
  586.6 128.7 %reduce-scatter.23.cloned.1.call-start = ((), (), s32[]{:S(2)}) async-start(), calls=%async_computation.17 | async-start | bytes 294912 | tf_op jit(solution)/shard_map/reduce_scatter | solution.py:199
Sparse Core Ops, SparseCore 0:
  61.8 60.4 reduce-scatter.12
  153.5 35.1 reduce-scatter.14
  237.7 64.3 reduce-scatter.24
  330.8 35.5 reduce-scatter.16
  410.9 60.4 reduce-scatter.18
  502.5 35.1 reduce-scatter.20
  586.7 64.4 reduce-scatter.26
  679.8 35.4 reduce-scatter.22
